TPU v7x, 32 devices: a whole 2x2x4 slice. The times are simulated.
32 devices in a mesh: fsdp: 8 (over y, x, core), dp: 4 (over z).
Axes of the slice: x: 2, y: 2, z: 4, core: 2. Of those that a mesh axis runs over, the one named last changes fastest.
Arguments:
- tokens: bfloat16 [131072, 1024], P(('fsdp', 'dp')), may hold values from -6 to 6
- cotangent: bfloat16 [131072, 1024], P(('fsdp', 'dp')), may hold values from -6 to 6
- lengths: int32 [256], P(('fsdp', 'dp')), may hold values from 8 to 2048, as said below
- selected: int32 [16384], P(('fsdp', 'dp')), may hold values from 0 to 4095, as said below
- attn_in: bfloat16 [1024, 3072], P('fsdp'), may hold values from -0.1875 to 0.1875
- attn_out: bfloat16 [1024, 1024], P('fsdp'), may hold values from -0.75 to 0.75
- mlp_in: bfloat16 [1024, 4096], P('fsdp'), may hold values from -0.1875 to 0.1875
- mlp_out: bfloat16 [4096, 1024], P('fsdp'), may hold values from -0.09375 to 0.09375
- norm_attn: bfloat16 [1024], P('fsdp'), may hold values from 0.5 to 1.5
- norm_mlp: bfloat16 [1024], P('fsdp'), may hold values from 0.5 to 1.5
- router: bfloat16 [1024], replicated, may hold values from -0.1875 to 0.1875
Outputs:
- output: bfloat16 [131072, 1024], P(('fsdp', 'dp'))
- grad_tokens: bfloat16 [131072, 1024], P(('fsdp', 'dp'))
- grad_attn_in: float32 [1024, 3072], P('fsdp')
- grad_attn_out: float32 [1024, 1024], P('fsdp')
- grad_mlp_in: float32 [1024, 4096], P('fsdp')
- grad_mlp_out: float32 [4096, 1024], P('fsdp')
- grad_norm_attn: float32 [1024], P('fsdp')
- grad_norm_mlp: float32 [1024], P('fsdp')
- grad_router: float32 [1024], replicated
Inputs may be any that keep to these rules, and one draw needn't show every extreme that they name: `lengths`: each aligned block of 8 entries (one device's sequences, in order) holds multiples of 8 that sum to 4096; exactly one of them equals 2048. `selected`: each aligned block of 512 entries lists distinct positions within its device's 4096 tokens in ascending order; a sequence of length L has exactly L / 8 of its positions listed.
All inputs are finite; a program needn't handle non-finite values.
Results may differ from a plain program's by a relative error of at most 0.014.
Values may be sent and summed in bfloat16 or wider, within the bound.
No kernel may reach another device: no remote copies, remote signals or barrier semaphores. Data moves between devices by JAX's collectives and lax.ppermute only.
A program may use at most 192 MiB of HBM per device.

v0:
```python
import numpy as np
import jax
import jax.numpy as jnp
from jax import lax
from jax.sharding import PartitionSpec as P

HEADS = 16
HEAD = 64
EPS = 1e-06
MASKED = -1e30


def rms_scale(values, gain_vec):
    return values * lax.rsqrt(jnp.mean(values * values, axis=-1, keepdims=True) + EPS) * gain_vec


def seq_mask(lengths, selected):
    seq_ends = jnp.cumsum(lengths)
    owner_seq = jnp.sum((selected[:, None] >= seq_ends[None, :]).astype(jnp.int32), axis=1)
    return (owner_seq[:, None] == owner_seq[None, :]) & (selected[None, :] <= selected[:, None])


def split_heads(matrix):
    return matrix.reshape(matrix.shape[0], HEADS, HEAD)


def masked_scores(query_heads, key_heads, allowed, score_scale):
    scores = (
        jnp.einsum("qhd,khd->hqk", query_heads, key_heads, preferred_element_type=jnp.float32)
        * score_scale
    )
    return jnp.where(allowed[None], scores, MASKED)


def plane_layout(mesh):
    devs = np.asarray(mesh.devices)
    if devs.ndim != 2 or devs.shape[0] != 8:
        return False
    try:
        for j in range(devs.shape[1]):
            for i in range(8):
                here = devs[i, j]
                mate = devs[i ^ 1, j]
                if (
                    tuple(mate.coords) != tuple(here.coords)
                    or mate.core_on_chip == here.core_on_chip
                ):
                    return False
                steps = []
                for bit in (2, 4):
                    other = devs[i ^ bit, j]
                    if other.core_on_chip != here.core_on_chip:
                        return False
                    diff = [abs(a - b) for a, b in zip(other.coords, here.coords)]
                    if sorted(diff) != [0] * (len(diff) - 1) + [1]:
                        return False
                    steps.append(diff.index(1))
                if steps[0] == steps[1]:
                    return False
    except AttributeError:
        return False
    return True


def swap_pairs(bit, size):
    return [(i, i ^ bit) for i in range(size)]


def plane_reduce(grad):
    rows, cols = grad.shape
    part = rows // 8
    half = part // 2
    me = lax.axis_index("fsdp")
    core = me % 2
    xi = me // 2 % 2
    yi = me // 4
    blocks = grad.reshape(4, 2, part, cols)
    keep = lax.dynamic_index_in_dim(blocks, core, axis=1, keepdims=False)
    send = lax.dynamic_index_in_dim(blocks, 1 - core, axis=1, keepdims=False)
    got = lax.ppermute(send.astype(jnp.bfloat16), "fsdp", swap_pairs(1, 8))
    chip = keep + got.astype(jnp.float32)

    def pick(y, x):
        return lax.dynamic_index_in_dim(chip, y * 2 + x, axis=0, keepdims=False)

    own = pick(yi, xi)
    to_x = pick(yi, 1 - xi)
    to_y = pick(1 - yi, xi)
    to_d = pick(1 - yi, 1 - xi)
    first_x = lax.ppermute(
        jnp.stack([to_x[:half], to_d[:half]]).astype(jnp.bfloat16), "fsdp", swap_pairs(2, 8)
    ).astype(jnp.float32)
    first_y = lax.ppermute(
        jnp.stack([to_y[half:], to_d[half:]]).astype(jnp.bfloat16), "fsdp", swap_pairs(4, 8)
    ).astype(jnp.float32)
    own_a = own[:half] + first_x[0]
    pass_a = to_y[:half] + first_x[1]
    own_b = own[half:] + first_y[0]
    pass_b = to_x[half:] + first_y[1]
    second_y = lax.ppermute(pass_a.astype(jnp.bfloat16), "fsdp", swap_pairs(4, 8)).astype(
        jnp.float32
    )
    second_x = lax.ppermute(pass_b.astype(jnp.bfloat16), "fsdp", swap_pairs(2, 8)).astype(
        jnp.float32
    )
    shard = jnp.concatenate([own_a + second_y, own_b + second_x], axis=0)
    return lax.psum(shard.astype(jnp.bfloat16), "dp").astype(jnp.float32)


def plain_reduce(grad):
    shard = lax.psum_scatter(grad.astype(jnp.bfloat16), "fsdp", scatter_dimension=0, tiled=True)
    return lax.psum(shard, "dp").astype(jnp.float32)


def make_per_device(reduce_grad):

    def per_device(
        tokens,
        cotangent,
        lengths,
        selected,
        attn_in,
        attn_out,
        mlp_in,
        mlp_out,
        norm_attn,
        norm_mlp,
        router,
    ):
        model_width = tokens.shape[1]
        row_count = selected.shape[0]
        score_scale = HEAD ** (-0.5)
        w_qkv, gain_attn = (
            lax.all_gather(attn_in, "fsdp", axis=0, tiled=True),
            lax.all_gather(norm_attn, "fsdp", axis=0, tiled=True),
        )
        w_out = lax.all_gather(attn_out, "fsdp", axis=0, tiled=True)
        w_in, gain_mlp = (
            lax.all_gather(mlp_in, "fsdp", axis=0, tiled=True),
            lax.all_gather(norm_mlp, "fsdp", axis=0, tiled=True),
        )
        w_down = lax.all_gather(mlp_out, "fsdp", axis=0, tiled=True)
        gain_one = gain_attn.astype(jnp.float32)
        gain_two = gain_mlp.astype(jnp.float32)
        positions = lax.broadcasted_iota(jnp.int32, (row_count, tokens.shape[0]), 1)
        select = (selected[:, None] == positions).astype(jnp.bfloat16)
        routed = jnp.dot(select, tokens, preferred_element_type=jnp.float32)
        routed_low = routed.astype(jnp.bfloat16)
        router_rate = jnp.dot(routed_low, router, preferred_element_type=jnp.float32)
        allowed = seq_mask(lengths, selected)
        normed_float, norm_pull = jax.vjp(rms_scale, routed, gain_one)
        normed = normed_float.astype(jnp.bfloat16)
        qkv = jnp.dot(normed, w_qkv, preferred_element_type=jnp.float32).astype(jnp.bfloat16)
        query_heads = split_heads(qkv[:, :model_width])
        key_heads = split_heads(qkv[:, model_width : 2 * model_width])
        value_heads = split_heads(qkv[:, 2 * model_width :])
        scores = masked_scores(query_heads, key_heads, allowed, score_scale)
        highest = jnp.max(scores, axis=-1, keepdims=True)
        exponent = jnp.exp(scores - highest)
        row_total = jnp.sum(exponent, axis=-1, keepdims=True)
        probabilities = (exponent / row_total).astype(jnp.bfloat16)
        log_total = highest + jnp.log(row_total)
        attn_mix = jnp.einsum(
            "hqk,khd->qhd", probabilities, value_heads, preferred_element_type=jnp.float32
        )
        attn_mix = attn_mix.reshape(row_count, model_width).astype(jnp.bfloat16)
        attended = jnp.dot(attn_mix, w_out, preferred_element_type=jnp.float32)
        middle = routed + attended
        normed_two_float, middle_pull = jax.vjp(rms_scale, middle, gain_two)
        normed_two = normed_two_float.astype(jnp.bfloat16)
        pre_gelu = jnp.dot(normed_two, w_in, preferred_element_type=jnp.float32)
        active_float, gelu_pull = jax.vjp(jax.nn.gelu, pre_gelu)
        active = active_float.astype(jnp.bfloat16)
        expanded = jnp.dot(active, w_down, preferred_element_type=jnp.float32)
        update = attended + expanded
        branch = (router_rate[:, None] * update).astype(jnp.bfloat16)
        output = (
            tokens.astype(jnp.float32)
            + jnp.einsum("kt,kd->td", select, branch, preferred_element_type=jnp.float32)
        ).astype(jnp.bfloat16)
        cot_rows = jnp.dot(select, cotangent, preferred_element_type=jnp.float32)
        grad_rate = jnp.sum(cot_rows * update, axis=-1)
        grad_update = cot_rows * router_rate[:, None]
        grad_expanded = grad_update.astype(jnp.bfloat16)
        grad_down = jnp.einsum(
            "kf,kd->fd", active, grad_expanded, preferred_element_type=jnp.float32
        )
        shard_down = reduce_grad(grad_down)
        grad_active = jnp.einsum(
            "kd,fd->kf", grad_expanded, w_down, preferred_element_type=jnp.float32
        )
        (grad_inner_float,) = gelu_pull(grad_active)
        grad_inner = grad_inner_float.astype(jnp.bfloat16)
        grad_up = jnp.einsum(
            "kd,kf->df", normed_two, grad_inner, preferred_element_type=jnp.float32
        )
        shard_up = reduce_grad(grad_up)
        grad_normed_two = jnp.einsum(
            "kf,df->kd", grad_inner, w_in, preferred_element_type=jnp.float32
        )
        grad_middle, grad_gain_two = middle_pull(grad_normed_two)
        grad_attended = (grad_update + grad_middle).astype(jnp.bfloat16)
        grad_proj = jnp.einsum(
            "ka,kd->ad", attn_mix, grad_attended, preferred_element_type=jnp.float32
        )
        shard_proj = reduce_grad(grad_proj)
        grad_mix = jnp.einsum(
            "kd,ad->ka", grad_attended, w_out, preferred_element_type=jnp.float32
        ).astype(jnp.bfloat16)
        grad_mix_heads = split_heads(grad_mix)
        scores_again = masked_scores(query_heads, key_heads, allowed, score_scale)
        prob_float = jnp.where(allowed[None], jnp.exp(scores_again - log_total), 0.0)
        grad_probs = jnp.einsum(
            "qhd,khd->hqk", grad_mix_heads, value_heads, preferred_element_type=jnp.float32
        )
        row_delta = jnp.sum(prob_float * grad_probs, axis=-1, keepdims=True)
        grad_scores = (prob_float * (grad_probs - row_delta)).astype(jnp.bfloat16)
        prob_low = prob_float.astype(jnp.bfloat16)
        grad_query = (
            jnp.einsum("hqk,khd->qhd", grad_scores, key_heads, preferred_element_type=jnp.float32)
            * score_scale
        )
        grad_key = (
            jnp.einsum("hqk,qhd->khd", grad_scores, query_heads, preferred_element_type=jnp.float32)
            * score_scale
        )
        grad_value = jnp.einsum(
            "hqk,qhd->khd", prob_low, grad_mix_heads, preferred_element_type=jnp.float32
        )
        grad_qkv = jnp.concatenate(
            [
                grad_query.reshape(row_count, model_width),
                grad_key.reshape(row_count, model_width),
                grad_value.reshape(row_count, model_width),
            ],
            axis=1,
        ).astype(jnp.bfloat16)
        grad_proj_in = jnp.einsum("kd,ke->de", normed, grad_qkv, preferred_element_type=jnp.float32)
        shard_qkv = reduce_grad(grad_proj_in)
        grad_normed = jnp.einsum("ke,de->kd", grad_qkv, w_qkv, preferred_element_type=jnp.float32)
        grad_routed_norm, grad_gain_one = norm_pull(grad_normed)
        grad_routed = (
            grad_routed_norm + grad_middle + grad_rate[:, None] * router.astype(jnp.float32)
        ).astype(jnp.bfloat16)
        grad_tokens = (
            cotangent.astype(jnp.float32)
            + jnp.einsum("kt,kd->td", select, grad_routed, preferred_element_type=jnp.float32)
        ).astype(jnp.bfloat16)
        router_local = jnp.dot(grad_rate, routed, precision=lax.Precision.HIGHEST)
        small = lax.psum(
            jnp.concatenate([grad_gain_one, grad_gain_two, router_local]), ("fsdp", "dp")
        )
        gain_part = grad_gain_one.shape[0] // lax.axis_size("fsdp")
        me = lax.axis_index("fsdp")
        shard_gain_one = lax.dynamic_slice_in_dim(small, me * gain_part, gain_part)
        shard_gain_two = lax.dynamic_slice_in_dim(
            small, grad_gain_one.shape[0] + me * gain_part, gain_part
        )
        grad_router = small[2 * grad_gain_one.shape[0] :]
        return (
            output,
            grad_tokens,
            shard_qkv,
            shard_proj,
            shard_up,
            shard_down,
            shard_gain_one,
            shard_gain_two,
            grad_router,
        )

    return per_device


def solution(mesh):
    placed = (
        P(("fsdp", "dp"), None),
        P(("fsdp", "dp"), None),
        P(("fsdp", "dp")),
        P(("fsdp", "dp")),
        P("fsdp", None),
        P("fsdp", None),
        P("fsdp", None),
        P("fsdp", None),
        P("fsdp"),
        P("fsdp"),
        P(),
    )
    reduce_grad = plane_reduce if plane_layout(mesh) else plain_reduce
    return jax.shard_map(
        make_per_device(reduce_grad),
        mesh=mesh,
        in_specs=placed,
        out_specs=(
            P(("fsdp", "dp"), None),
            P(("fsdp", "dp"), None),
            P("fsdp", None),
            P("fsdp", None),
            P("fsdp", None),
            P("fsdp", None),
            P("fsdp"),
            P("fsdp"),
            P(),
        ),
        check_vma=False,
    )
```

profile of v0, /device:TPU:0, one launch (start us, length us, event | category | flops | bytes accessed | tf_op | source)
XLA Modules:
  0.0 639.2 jit_solution(1268586833503978225)
XLA Ops:
  12.9 10.4 %all-gather = bf16[8,1,128]{2,1,0:T(2,128)(2,1)S(1)} all-gather(bf16[1,1,128]{2,1,0:T(2,128)(2,1)} %bitcast.194), channel_id=1, replica_groups=mesh['fsdp'=8,'dp'=4] {'fsdp'}, dimensions={0}, use_global_device_ids=true | all-gather | bytes 2304 | tf_op jit(solution)/shard_map/all_gather | solution.py:135
  23.3 8.8 %all-gather.1 = bf16[8,1,128]{2,1,0:T(2,128)(2,1)S(1)} all-gather(bf16[1,1,128]{2,1,0:T(2,128)(2,1)} %bitcast.195), channel_id=1, replica_groups=mesh['fsdp'=8,'dp'=4] {'fsdp'}, dimensions={0}, use_global_device_ids=true | all-gather | bytes 2304 | tf_op jit(solution)/shard_map/all_gather | solution.py:140
  41.4 9.3 %fusion.12 = f32[512,1024]{1,0:T(8,128)} fusion(bf16[4096,1024]{1,0:T(8,128)(2,1)} %param.12, s32[512]{0:T(512)S(1)} %copy-done.15), kind=kOutput, calls=%fused_computation.28 | convolution fusion | flops 4297064448 | bytes 10487808 | tf_op jit(solution)/shard_map/dot_general | solution.py:181
  72.4 8.8 %fusion.1 = (f32[16,512]{1,0:T(8,128)S(1)}, f32[16,512,512]{1,2,0:T(8,128)}) fusion(pred[512,512]{0,1:T(8,128)(4,1)S(1)} %compare_and_fusion, bf16[512,16,64]{0,2,1:T(8,128)(2,1)} %bitcast.161, bf16[512,16,64]{0,2,1:T(8,128)(2,1)S(1)} %bitcast.159), kind=kOutput, calls=%fused_computation.11 | convolution fusion | flops 549445632 | bytes 19169280 | tf_op jit(solution)/shard_map/qhd,khd->hqk/dot_general | solution.py:29
  81.3 9.3 %fusion = f32[16,512]{1,0:T(8,128)S(1)} fusion(f32[16,512,512]{1,2,0:T(8,128)} %get-tuple-element.61, f32[16,512]{1,0:T(8,128)S(1)} %get-tuple-element.60, pred[512,512]{0,1:T(8,128)(4,1)S(1)} %compare_and_fusion), kind=kLoop, calls=%fused_computation.8 | loop fusion | flops 16769024 | bytes 17104896 | tf_op jit(solution)/shard_map/reduce_sum | solution.py:160
  90.6 9.5 %fusion.26 = bf16[16,64,512]{2,1,0:T(8,128)(2,1)} fusion(bf16[512,16,64]{0,2,1:T(8,128)(2,1)} %bitcast.175, f32[16,512,512]{1,2,0:T(8,128)} %get-tuple-element.61, f32[16,512]{1,0:T(8,128)S(1)} %fusion, f32[16,512]{1,0:T(8,128)S(1)} %get-tuple-element.60, pred[512,512]{0,1:T(8,128)(4,1)S(1)} %compare_and_fusion), kind=kOutput, calls=%fused_computation.68 | convolution fusion | flops 558366720 | bytes 19202048 | tf_op jit(solution)/shard_map/hqk,khd->qhd/dot_general | solution.py:163
  105.3 38.6 %all-gather.11.cloned.1.call-done = bf16[1024,4096]{1,0:T(8,128)(2,1)} async-done(((bf16[128,4096]{1,0:T(8,128)(2,1)}), bf16[1024,4096]{1,0:T(8,128)(2,1)}) %all-gather.11.cloned.1.call-update) | async-done | bytes 8388624 | tf_op jit(solution)/shard_map/all_gather | solution.py:139
  155.4 9.2 %fusion.93 = f32[4096,1024]{1,0:T(8,128)} fusion(f32[512,1024]{1,0:T(8,128)S(1)} %copy-done.40, f32[512]{0:T(512)S(1)} %bitcast.189, f32[512,4096]{1,0:T(8,128)S(1)} %fusion.96), kind=kOutput, calls=%fused_computation.178 | convolution fusion | flops 4314890240 | bytes 27265024 | tf_op jit(solution)/shard_map/kf,kd->fd/dot_general | solution.py:185
  164.7 35.3 %all-gather.13.cloned.1.call-done = bf16[4096,1024]{1,0:T(8,128)(2,1)} async-done(((bf16[512,1024]{1,0:T(8,128)(2,1)}), bf16[4096,1024]{1,0:T(8,128)(2,1)}) %all-gather.13.cloned.1.call-update) | async-done | bytes 8388624 | tf_op jit(solution)/shard_map/all_gather | solution.py:142
  199.9 13.3 %fusion.8 = bf16[512,4096]{1,0:T(8,128)(2,1)S(1)} fusion(f32[512,4096]{1,0:T(8,128)} %copy-done.39, bf16[4096,1024]{1,0:T(8,128)(2,1)} %all-gather.13.cloned.1.call-done, f32[512,1024]{1,0:T(8,128)} %fusion.12, f32[512]{0:T(512)S(1)} %bitcast.190), kind=kOutput, calls=%fused_computation.18 | convolution fusion | flops 4337958912 | bytes 23070720 | tf_op jit(solution)/shard_map/kd,fd->kf/dot_general | solution.py:189
  215.3 8.4 %fusion.95 = f32[1024,4096]{1,0:T(8,128)} fusion(bf16[512,4096]{1,0:T(8,128)(2,1)S(1)} %fusion.8, f32[512,1024]{1,0:T(8,128)S(1)} %copy-done.4, f32[1024]{0:T(1024)S(1)} %bitcast.185, f32[512]{0:T(512)S(1)} %fusion.85), kind=kOutput, calls=%fused_computation.180 | convolution fusion | flops 4296540160 | bytes 23074816 | tf_op jit(solution)/shard_map/kd,kf->df/dot_general | solution.py:194
  223.7 11.5 %multiply_reduce_fusion.1 = (f32[1024]{0:T(1024)}, f32[512]{0:T(512)S(1)}, f32[512,1024]{1,0:T(8,128)}) fusion(f32[512,1024]{1,0:T(8,128)S(1)} %copy-done.4, f32[512]{0:T(512)S(1)} %fusion.85, f32[1024]{0:T(1024)S(1)} %bitcast.186, bf16[512,4096]{1,0:T(8,128)(2,1)} %copy-done.38, bf16[1024,4096]{1,0:T(8,128)(2,1)} %all-gather.11.cloned.1.call-done), kind=kOutput, calls=%fused_computation.49 | convolution fusion | flops 4298111488 | bytes 16789504 | tf_op jit(solution)/shard_map/kf,df->kd/dot_general | solution.py:198
  235.3 10.3 %multiply_reduce_fusion.3 = (f32[512]{0:T(512)S(1)}, bf16[512,1024]{1,0:T(8,128)(2,1)S(1)}, f32[512,1024]{1,0:T(8,128)}) fusion(f32[512,1024]{1,0:T(8,128)S(1)} %copy-done.41, f32[512,1024]{1,0:T(8,128)S(1)} %copy-done.4, f32[512]{0:T(512)S(1)} %multiply_multiply_fusion.3, f32[512]{0:T(512)S(1)} %fusion.85, f32[512,1024]{1,0:T(8,128)} %get-tuple-element.63, ...), kind=kOutput, calls=%fused_computation.54 | convolution fusion | flops 4319608320 | bytes 28323840 | tf_op jit(solution)/shard_map/dot_general | solution.py:174
  251.2 11.5 %fusion.27 = bf16[16,64,512]{2,1,0:T(8,128)(2,1)} fusion(bf16[512,16,64]{0,2,1:T(8,128)(2,1)} %bitcast.177, f32[16,512]{1,0:T(8,128)S(1)} %log_add_fusion, f32[16,512,512]{1,2,0:T(8,128)} %get-tuple-element.61, pred[512,512]{0,1:T(8,128)(4,1)S(1)} %compare_and_fusion), kind=kOutput, calls=%fused_computation.70 | convolution fusion | flops 558366720 | bytes 19169280 | tf_op jit(solution)/shard_map/hqk,qhd->khd/dot_general | solution.py:227
  262.8 12.5 %multiply_reduce_fusion = (f32[16,512]{1,0:T(8,128)S(1)}, f32[16,512,512]{1,2,0:T(8,128)}) fusion(f32[16,512]{1,0:T(8,128)S(1)} %log_add_fusion, f32[16,512,512]{1,2,0:T(8,128)} %get-tuple-element.61, pred[512,512]{0,1:T(8,128)(4,1)S(1)} %compare_and_fusion, bf16[512,16,64]{0,2,1:T(8,128)(2,1)S(1)} %bitcast.178, bf16[512,16,64]{0,2,1:T(8,128)(2,1)S(1)} %bitcast.176), kind=kOutput, calls=%fused_computation.2 | convolution fusion | flops 562028544 | bytes 35979264 | tf_op jit(solution)/shard_map/qhd,khd->hqk/dot_general | solution.py:213
  275.2 12.6 %multiply_convert_fusion = bf16[16,512,512]{1,2,0:T(8,128)(2,1)S(1)} fusion(f32[16,512,512]{1,2,0:T(8,128)} %get-tuple-element.66, f32[16,512]{1,0:T(8,128)S(1)} %get-tuple-element.65, f32[16,512]{1,0:T(8,128)S(1)} %log_add_fusion, f32[16,512,512]{1,2,0:T(8,128)} %get-tuple-element.61, pred[512,512]{0,1:T(8,128)(4,1)S(1)} %compare_and_fusion), kind=kLoop, calls=%fused_computation.1 | loop fusion | flops 29360128 | bytes 42270720 | tf_op jit(solution)/shard_map/convert_element_type | solution.py:217
  313.7 9.0 %multiply_reduce_fusion.2 = (f32[1024]{0:T(1024)}, f32[512]{0:T(512)S(1)}, f32[512,1024]{1,0:T(8,128)}) fusion(f32[512,1024]{1,0:T(8,128)S(1)} %get-tuple-element.59, f32[512]{0:T(512)S(1)} %copy-done.34, f32[1024]{0:T(1024)S(1)} %bitcast.182, bf16[1024,3072]{1,0:T(8,128)(2,1)} %all-gather.7.cloned.1.call-done, bf16[512,1024]{0,1:T(8,128)(2,1)} %bitcast.201, ...), kind=kOutput, calls=%fused_computation.50 | convolution fusion | flops 3233806848 | bytes 13643776 | tf_op jit(solution)/shard_map/ke,de->kd/dot_general | solution.py:240
  346.4 52.0 %psum.39 = f32[3072]{0:T(1024)} all-reduce(f32[3072]{0:T(1024)S(1)} %pad_maximum_fusion.15), channel_id=1, replica_groups=mesh['fsdp'=8,'dp'=4] {'fsdp','dp'}, use_global_device_ids=true, to_apply=%region_16.17 | all-reduce | flops 3072 | bytes 24576 | tf_op jit(solution)/shard_map/psum | solution.py:250
  419.7 10.3 %bitcast_add_fusion = f32[4,512,1024]{2,1,0:T(8,128)} fusion(bf16[4,512,1024]{2,1,0:T(8,128)(2,1)} %collective-permute-done.15, f32[4,2,512,1024]{3,2,1,0:T(8,128)} %bitcast.164, s32[]{:T(128)S(6)} %select_n.97), kind=kLoop, calls=%fused_computation.21 | loop fusion | flops 4194304 | bytes 20971524 | tf_op jit(solution)/shard_map/add | solution.py:81
  440.2 19.6 %collective-permute-done.18 = bf16[2,256,1024]{2,1,0:T(8,128)(2,1)S(1)} collective-permute-done((bf16[2,256,1024]{2,1,0:T(8,128)(2,1)S(1)}, bf16[2,256,1024]{2,1,0:T(8,128)(2,1)S(1)}, u32[]{:S(2)}, u32[]{:S(2)}) %collective-permute-start.18) | collective-permute-done | bytes 1048608 | tf_op jit(solution)/shard_map/ppermute | solution.py:93
  463.5 18.8 %collective-permute-done.13 = bf16[2,64,4096]{2,1,0:T(8,128)(2,1)S(1)} collective-permute-done((bf16[2,64,4096]{2,1,0:T(8,128)(2,1)S(1)}, bf16[2,64,4096]{2,1,0:T(8,128)(2,1)S(1)}, u32[]{:S(2)}, u32[]{:S(2)}) %collective-permute-start.13) | collective-permute-done | bytes 1048608 | tf_op jit(solution)/shard_map/ppermute | solution.py:93
  504.3 10.0 %add_convert_fusion.1 = bf16[4096,1024]{1,0:T(8,128)(2,1)} fusion(bf16[4096,1024]{1,0:T(8,128)(2,1)} %param.11, s32[512]{0:T(512)S(1)} %copy-done.16, f32[512,1024]{1,0:T(8,128)} %get-tuple-element.64, f32[512]{0:T(512)S(1)} %bitcast.192), kind=kOutput, calls=%fused_computation.4 | convolution fusion | flops 4310695936 | bytes 18878464 | tf_op jit(solution)/shard_map/kt,kd->td/dot_general | solution.py:179
  514.4 11.7 %add_convert_fusion = bf16[4096,1024]{1,0:T(8,128)(2,1)} fusion(bf16[4096,1024]{1,0:T(8,128)(2,1)} %param.12, s32[512]{0:T(512)S(1)} %copy-done.16, f32[512,1024]{1,0:T(8,128)S(1)} %get-tuple-element.59, f32[512,1024]{1,0:T(8,128)S(1)} %copy-done.42, f32[1024]{0:T(1024)S(1)} %copy-done.19, f32[512]{0:T(512)S(1)} %copy-done.29, f32[512]{0:T(512)S(1)} %copy-done.32, ...), kind=kOutput, calls=%fused_computation | convolution fusion | flops 4316987392 | bytes 25190400 | tf_op jit(solution)/shard_map/kt,kd->td/dot_general | solution.py:247
  526.0 97.5 %all-reduce.3.cloned.1.call-done = (bf16[128,3072]{1,0:T(8,128)(2,1)}, bf16[128,1024]{1,0:T(8,128)(2,1)}, bf16[128,4096]{1,0:T(8,128)(2,1)}, bf16[512,1024]{1,0:T(8,128)(2,1)}) async-done(((bf16[128,3072]{1,0:T(8,128)(2,1)}, bf16[128,1024]{1,0:T(8,128)(2,1)}, bf16[128,4096]{1,0:T(8,128)(2,1)}, bf16[512,1024]{1,0:T(8,128)(2,1)}), (bf16[128,3072]{1,0:T(8,128)(2,1)}, bf16[128,1024]{1,0:T(8,128)(2,1)}, ...) | async-done | bytes 3145744 | tf_op jit(solution)/shard_map/psum | solution.py:107
  (230 shorter events, 175.8 us)
Async XLA Ops:
  7.2 50.9 %all-gather.7.cloned.1.call-start = ((), (), s32[]{:S(2)}) async-start(), calls=%async_computation | async-start | bytes 7077888 | tf_op jit(solution)/shard_map/all_gather | solution.py:134
  7.9 92.2 %all-gather.9.cloned.1.call-start = ((), (), s32[]{:S(2)}) async-start(), calls=%async_computation.1 | async-start | bytes 2359296 | tf_op jit(solution)/shard_map/all_gather | solution.py:137
  8.7 135.2 %all-gather.11.cloned.1.call-start = ((), (), s32[]{:S(2)}) async-start(), calls=%async_computation.2 | async-start | bytes 9437184 | tf_op jit(solution)/shard_map/all_gather | solution.py:139
  9.4 190.5 %all-gather.13.cloned.1.call-start = ((), (), s32[]{:S(2)}) async-start(), calls=%async_computation.3 | async-start | bytes 9437184 | tf_op jit(solution)/shard_map/all_gather | solution.py:142
  10.0 613.6 %all-reduce.3.cloned.1.call-start = ((), (), s32[]{:S(2)}) async-start(), calls=%async_computation.4 | async-start | bytes 6291456 | tf_op jit(solution)/shard_map/psum | solution.py:107
  293.4 29.2 %collective-permute-start.5 = (bf16[4,128,1024]{2,1,0:T(8,128)(2,1)S(1)}, bf16[4,128,1024]{2,1,0:T(8,128)(2,1)}, u32[]{:S(2)}, u32[]{:S(2)}) collective-permute-start(bf16[4,128,1024]{2,1,0:T(8,128)(2,1)S(1)} %fusion.32), channel_id=1, source_target_pairs={{0,4},{4,0},{8,12},{12,8},{16,20},{20,16},{24,28},{28,24},{1,5},{5... | collective-permute-start | bytes 3145736 | tf_op jit(solution)/shard_map/ppermute | solution.py:80
  299.8 119.9 %collective-permute-start.15 = (bf16[4,512,1024]{2,1,0:T(8,128)(2,1)}, bf16[4,512,1024]{2,1,0:T(8,128)(2,1)}, u32[]{:S(2)}, u32[]{:S(2)}) collective-permute-start(bf16[4,512,1024]{2,1,0:T(8,128)(2,1)} %fusion.17), channel_id=1, source_target_pairs={{0,4},{4,0},{8,12},{12,8},{16,20},{20,16},{24,28},{28,24},{1,5},{5... | collective-permute-start | bytes 12582920 | tf_op jit(solution)/shard_map/ppermute | solution.py:80
  307.1 27.8 %collective-permute-start = (bf16[4,128,3072]{2,1,0:T(8,128)(2,1)}, bf16[4,128,3072]{2,1,0:T(8,128)(2,1)}, u32[]{:S(2)}, u32[]{:S(2)}) collective-permute-start(bf16[4,128,3072]{2,1,0:T(8,128)(2,1)} %fusion.22), channel_id=1, source_target_pairs={{0,4},{4,0},{8,12},{12,8},{16,20},{20,16},{24,28},{28,24},{1,5},{5... | collective-permute-start | bytes 9437192 | tf_op jit(solution)/shard_map/ppermute | solution.py:80
  313.4 98.5 %collective-permute-start.10 = (bf16[4,128,4096]{2,1,0:T(8,128)(2,1)}, bf16[4,128,4096]{2,1,0:T(8,128)(2,1)}, u32[]{:S(2)}, u32[]{:S(2)}) collective-permute-start(bf16[4,128,4096]{2,1,0:T(8,128)(2,1)} %fusion.16), channel_id=1, source_target_pairs={{0,4},{4,0},{8,12},{12,8},{16,20},{20,16},{24,28},{28,24},{1,5},{5... | collective-permute-start | bytes 12582920 | tf_op jit(solution)/shard_map/ppermute | solution.py:80
  324.4 8.5 %collective-permute-start.8 = (bf16[2,64,1024]{2,1,0:T(8,128)(2,1)S(1)}, bf16[2,64,1024]{2,1,0:T(8,128)(2,1)S(1)}, u32[]{:S(2)}, u32[]{:S(2)}) collective-permute-start(bf16[2,64,1024]{2,1,0:T(8,128)(2,1)S(1)} %pad_maximum_fusion.13), channel_id=1, source_target_pairs={{0,16},{4,20},{8,24},{12,28},{16,0},{20,4},{24,8},{28,12},{1,17},{... | collective-permute-start | bytes 786440 | tf_op jit(solution)/shard_map/ppermute | solution.py:93
  334.0 11.3 %collective-permute-start.7 = (bf16[64,1024]{1,0:T(8,128)(2,1)S(1)}, bf16[64,1024]{1,0:T(8,128)(2,1)S(1)}, u32[]{:S(2)}, u32[]{:S(2)}) collective-permute-start(bf16[64,1024]{1,0:T(8,128)(2,1)S(1)} %get-tuple-element.42), channel_id=1, source_target_pairs={{0,16},{4,20},{8,24},{12,28},{16,0},{20,4},{24,8},{28,12},{1,17},{... | collective-permute-start | bytes 393224 | tf_op jit(solution)/shard_map/ppermute | solution.py:100
  341.7 61.2 %collective-permute-start.3 = (bf16[2,64,3072]{2,1,0:T(8,128)(2,1)}, bf16[2,64,3072]{2,1,0:T(8,128)(2,1)}, u32[]{:S(2)}, u32[]{:S(2)}) collective-permute-start(bf16[2,64,3072]{2,1,0:T(8,128)(2,1)} %pad_maximum_fusion.10), channel_id=1, source_target_pairs={{0,16},{4,20},{8,24},{12,28},{16,0},{20,4},{24,8},{28,12},{1,17},{... | collective-permute-start | bytes 2359304 | tf_op jit(solution)/shard_map/ppermute | solution.py:93
  343.8 60.4 %collective-permute-start.1 = (bf16[2,64,3072]{2,1,0:T(8,128)(2,1)}, bf16[2,64,3072]{2,1,0:T(8,128)(2,1)}, u32[]{:S(2)}, u32[]{:S(2)}) collective-permute-start(bf16[2,64,3072]{2,1,0:T(8,128)(2,1)} %pad_maximum_fusion.9), channel_id=1, source_target_pairs={{0,8},{4,12},{8,0},{12,4},{16,24},{20,28},{24,16},{28,20},{1,9},{5... | collective-permute-start | bytes 2359304 | tf_op jit(solution)/shard_map/ppermute | solution.py:90
  345.3 55.7 %collective-permute-start.9 = (bf16[64,1024]{1,0:T(8,128)(2,1)S(1)}, bf16[64,1024]{1,0:T(8,128)(2,1)S(1)}, u32[]{:S(2)}, u32[]{:S(2)}) collective-permute-start(bf16[64,1024]{1,0:T(8,128)(2,1)S(1)} %get-tuple-element.43), channel_id=1, source_target_pairs={{0,8},{4,12},{8,0},{12,4},{16,24},{20,28},{24,16},{28,20},{1,9},{5... | collective-permute-start | bytes 393224 | tf_op jit(solution)/shard_map/ppermute | solution.py:103
  408.0 29.2 %collective-permute-start.2 = (bf16[64,3072]{1,0:T(8,128)(2,1)}, bf16[64,3072]{1,0:T(8,128)(2,1)S(1)}, u32[]{:S(2)}, u32[]{:S(2)}) collective-permute-start(bf16[64,3072]{1,0:T(8,128)(2,1)} %get-tuple-element.33), channel_id=1, source_target_pairs={{0,16},{4,20},{8,24},{12,28},{16,0},{20,4},{24,8},{28,12},{1,17},{... | collective-permute-start | bytes 1179656 | tf_op jit(solution)/shard_map/ppermute | solution.py:100
  410.7 27.8 %collective-permute-start.4 = (bf16[64,3072]{1,0:T(8,128)(2,1)}, bf16[64,3072]{1,0:T(8,128)(2,1)}, u32[]{:S(2)}, u32[]{:S(2)}) collective-permute-start(bf16[64,3072]{1,0:T(8,128)(2,1)} %get-tuple-element.34), channel_id=1, source_target_pairs={{0,8},{4,12},{8,0},{12,4},{16,24},{20,28},{24,16},{28,20},{1,9},{5... | collective-permute-start | bytes 1179656 | tf_op jit(solution)/shard_map/ppermute | solution.py:103
  433.7 26.1 %collective-permute-start.18 = (bf16[2,256,1024]{2,1,0:T(8,128)(2,1)S(1)}, bf16[2,256,1024]{2,1,0:T(8,128)(2,1)S(1)}, u32[]{:S(2)}, u32[]{:S(2)}) collective-permute-start(bf16[2,256,1024]{2,1,0:T(8,128)(2,1)S(1)} %pad_maximum_fusion.7), channel_id=1, source_target_pairs={{0,16},{4,20},{8,24},{12,28},{16,0},{20,4},{24,8},{28,12},{1,17},{... | collective-permute-start | bytes 3145736 | tf_op jit(solution)/shard_map/ppermute | solution.py:93
  434.3 26.1 %collective-permute-start.16 = (bf16[2,256,1024]{2,1,0:T(8,128)(2,1)S(1)}, bf16[2,256,1024]{2,1,0:T(8,128)(2,1)S(1)}, u32[]{:S(2)}, u32[]{:S(2)}) collective-permute-start(bf16[2,256,1024]{2,1,0:T(8,128)(2,1)S(1)} %pad_maximum_fusion.6), channel_id=1, source_target_pairs={{0,8},{4,12},{8,0},{12,4},{16,24},{20,28},{24,16},{28,20},{1,9},{5... | collective-permute-start | bytes 3145736 | tf_op jit(solution)/shard_map/ppermute | solution.py:90
  435.0 47.3 %collective-permute-start.13 = (bf16[2,64,4096]{2,1,0:T(8,128)(2,1)S(1)}, bf16[2,64,4096]{2,1,0:T(8,128)(2,1)S(1)}, u32[]{:S(2)}, u32[]{:S(2)}) collective-permute-start(bf16[2,64,4096]{2,1,0:T(8,128)(2,1)S(1)} %pad_maximum_fusion.4), channel_id=1, source_target_pairs={{0,16},{4,20},{8,24},{12,28},{16,0},{20,4},{24,8},{28,12},{1,17},{... | collective-permute-start | bytes 3145736 | tf_op jit(solution)/shard_map/ppermute | solution.py:93
  437.2 45.6 %collective-permute-start.11 = (bf16[2,64,4096]{2,1,0:T(8,128)(2,1)S(1)}, bf16[2,64,4096]{2,1,0:T(8,128)(2,1)S(1)}, u32[]{:S(2)}, u32[]{:S(2)}) collective-permute-start(bf16[2,64,4096]{2,1,0:T(8,128)(2,1)S(1)} %pad_maximum_fusion.3), channel_id=1, source_target_pairs={{0,8},{4,12},{8,0},{12,4},{16,24},{20,28},{24,16},{28,20},{1,9},{5... | collective-permute-start | bytes 3145736 | tf_op jit(solution)/shard_map/ppermute | solution.py:90
  460.9 32.6 %collective-permute-start.17 = (bf16[256,1024]{1,0:T(8,128)(2,1)S(1)}, bf16[256,1024]{1,0:T(8,128)(2,1)S(1)}, u32[]{:S(2)}, u32[]{:S(2)}) collective-permute-start(bf16[256,1024]{1,0:T(8,128)(2,1)S(1)} %get-tuple-element.21), channel_id=1, source_target_pairs={{0,16},{4,20},{8,24},{12,28},{16,0},{20,4},{24,8},{28,12},{1,17},{... | collective-permute-start | bytes 1572872 | tf_op jit(solution)/shard_map/ppermute | solution.py:100
  462.6 31.4 %collective-permute-start.19 = (bf16[256,1024]{1,0:T(8,128)(2,1)S(1)}, bf16[256,1024]{1,0:T(8,128)(2,1)S(1)}, u32[]{:S(2)}, u32[]{:S(2)}) collective-permute-start(bf16[256,1024]{1,0:T(8,128)(2,1)S(1)} %get-tuple-element.22), channel_id=1, source_target_pairs={{0,8},{4,12},{8,0},{12,4},{16,24},{20,28},{24,16},{28,20},{1,9},{5... | collective-permute-start | bytes 1572872 | tf_op jit(solution)/shard_map/ppermute | solution.py:103
  483.3 18.3 %collective-permute-start.12 = (bf16[64,4096]{1,0:T(8,128)(2,1)S(1)}, bf16[64,4096]{1,0:T(8,128)(2,1)S(1)}, u32[]{:S(2)}, u32[]{:S(2)}) collective-permute-start(bf16[64,4096]{1,0:T(8,128)(2,1)S(1)} %get-tuple-element.27), channel_id=1, source_target_pairs={{0,16},{4,20},{8,24},{12,28},{16,0},{20,4},{24,8},{28,12},{1,17},{... | collective-permute-start | bytes 1572872 | tf_op jit(solution)/shard_map/ppermute | solution.py:100
  485.0 17.7 %collective-permute-start.14 = (bf16[64,4096]{1,0:T(8,128)(2,1)S(1)}, bf16[64,4096]{1,0:T(8,128)(2,1)S(1)}, u32[]{:S(2)}, u32[]{:S(2)}) collective-permute-start(bf16[64,4096]{1,0:T(8,128)(2,1)S(1)} %get-tuple-element.28), channel_id=1, source_target_pairs={{0,8},{4,12},{8,0},{12,4},{16,24},{20,28},{24,16},{28,20},{1,9},{5... | collective-permute-start | bytes 1572872 | tf_op jit(solution)/shard_map/ppermute | solution.py:103
  (49 other events, 1060.1 us)
Sparse Core Ops, SparseCore 0:
  9.9 48.1 all-gather.6
  59.9 27.7 all-gather.8
  89.6 54.2 all-gather.10
  145.6 54.2 all-gather.12
  504.3 119.2 all-reduce.2
where the time goes:
time: 649 us; the launch traced here: 639 us
  waiting for transfers between devices  241 us (37%)
  matrix products  177 us (27%)
  other arithmetic  71.4 us (11%)
  blocking collectives  71.3 us (11%)
  local copies, waits for them, and re-layouts  43.3 us (7%)
  starting transfers between devices  20.8 us (3%)
  between operations  15.1 us (2%)
    psum x1, waiting for transfers between devices, plane_reduce(): return lax.psum(shard.astype(jnp.bfloat16), 'dp').astype(jnp.float32)  97.5 us
    psum x1, blocking collectives, per_device(): lax.psum(jnp.concatenate([grad_gain_one, grad_gain_two, router_local]), (...  52 us
    ppermute x4, waiting for transfers between devices, plane_reduce(): lax.ppermute(jnp.stack([to_y[half:], to_d[half:]]).astype(jnp.bfloat16),...  43.7 us
    all_gather x1, waiting for transfers between devices, per_device(): lax.all_gather(mlp_in, 'fsdp', axis=0, tiled=True)  38.6 us
    all_gather x1, waiting for transfers between devices, per_device(): w_down = lax.all_gather(mlp_out, 'fsdp', axis=0, tiled=True)  35.3 us
    add x4, other arithmetic, plane_reduce(): chip = keep + got.astype(jnp.float32)  20.5 us
    convert_element_type x4, local copies, waits for them, and re-layouts, plane_reduce(): got = lax.ppermute(send.astype(jnp.bfloat16), 'fsdp', swap_pairs(1, 8))  14.3 us
    dot_general x1, matrix products, per_device(): jnp.einsum('kd,fd->kf', grad_expanded, w_down, preferred_element_type=jnp...  13.3 us
  transfers between devices with their start and end apart: 25, of which 14 were waited for; matrix products, arithmetic and copies ran while one was open for 28% of the time, Pallas kernels for 0%

commit v1 on v0

--- a/solution.py
+++ b/solution.py
@@ -1,3 +1,4 @@
+import functools
 import numpy as np
 import jax
 import jax.numpy as jnp
@@ -8,6 +9,28 @@
 HEAD = 64
 EPS = 1e-06
 MASKED = -1e30
+
+
+def close_floor(local_array, peer_axis):
+    w2, r_now, f_now = (lax.axis_size(peer_axis), lax.axis_index(peer_axis), local_array.shape[0])
+    heap = list(map(lambda dd: (dd, (dd + 1) % w2), range(w2)))
+    rack = list(map(lambda dd: (dd, (dd - 1) % w2), range(w2)))
+    e_now = jnp.zeros(
+        (*local_array.shape[:0], w2 * f_now, *local_array.shape[1:]), local_array.dtype
+    )
+    e_now = lax.dynamic_update_slice_in_dim(e_now, local_array, r_now * f_now, axis=0)
+    m_next = now = local_array
+    x_new = w2 // 2
+    for tick in [*range(1, x_new + 1)]:
+        m_next = lax.ppermute(m_next, peer_axis, heap)
+        e_now = lax.dynamic_update_slice_in_dim(e_now, m_next, (r_now - tick) % w2 * f_now, axis=0)
+        if tick < w2 - x_new:
+            now = lax.ppermute(now, peer_axis, rack)
+            e_now = lax.dynamic_update_slice_in_dim(e_now, now, (r_now + tick) % w2 * f_now, axis=0)
+    return e_now
+
+
+perform_numbers = functools.partial(close_floor, peer_axis="fsdp")
 
 
 def rms_scale(values, gain_vec):
@@ -136,7 +159,7 @@
         )
         w_out = lax.all_gather(attn_out, "fsdp", axis=0, tiled=True)
         w_in, gain_mlp = (
-            lax.all_gather(mlp_in, "fsdp", axis=0, tiled=True),
+            perform_numbers(mlp_in),
             lax.all_gather(norm_mlp, "fsdp", axis=0, tiled=True),
         )
         w_down = lax.all_gather(mlp_out, "fsdp", axis=0, tiled=True)

time: 649 us -> 662 us (1.020)
  waiting for transfers between devices: 241 us -> 222 us
  local copies, waits for them, and re-layouts: 43.3 us -> 59.1 us
  blocking collectives: 71.3 us -> 85 us
    ppermute x0 -> x7, waiting for transfers between devices: none -> 54 us  [the longest x4 52.6 us: close_floor(): m_next = lax.ppermute(m_next, peer_axis, heap)]
    all_gather x1 -> x0, waiting for transfers between devices: 38.6 us -> none  [per_device(): lax.all_gather(mlp_in, 'fsdp', axis=0, tiled=True)]
    all_gather x1, waiting for transfers between devices: 35.3 us -> 0.02 us  [per_device(): w_down = lax.all_gather(mlp_out, 'fsdp', axis=0, tiled=True)]
    all_gather x1, blocking collectives: 10.4 us -> 36.3 us  [per_device(): lax.all_gather(norm_attn, 'fsdp', axis=0, tiled=True)]
    ppermute x4, waiting for transfers between devices: 12.6 us -> 27.9 us  [plane_reduce(): lax.ppermute(pass_a.astype(jnp.bfloat16), 'fsdp', swap_pairs(4, 8))]
    ppermute x4, waiting for transfers between devices: 43.7 us -> 29.8 us  [plane_reduce(): lax.ppermute(jnp.stack([to_y[half:], to_d[half:]]).astype(jnp.bfloat16),...]
    psum x1, blocking collectives: 52 us -> 39.7 us  [per_device(): lax.psum(jnp.concatenate([grad_gain_one, grad_gain_two, router_local]), (...]
    dynamic_update_slice x0 -> x8, local copies, waits for them, and re-layouts: none -> 12.1 us  [the longest x4 6.65 us: close_floor(): lax.dynamic_update_slice_in_dim(e_now, m_next, (r_now - tick) % w2 * f_no...]
  transfers between devices with their start and end apart: 25 -> 31, of which waited for: 14 -> 14; matrix products, arithmetic and copies ran while one was open for 28% -> 42% of each run, Pallas kernels for 0% -> 0%
where the time goes in v1:
time: 662 us; the launch traced here: 654 us
  waiting for transfers between devices  222 us (34%)
  matrix products  176 us (27%)
  blocking collectives  85 us (13%)
  other arithmetic  70.2 us (11%)
  local copies, waits for them, and re-layouts  59.1 us (9%)
  starting transfers between devices  26.6 us (4%)
  between operations  15.2 us (2%)
    psum x1, waiting for transfers between devices, plane_reduce(): return lax.psum(shard.astype(jnp.bfloat16), 'dp').astype(jnp.float32)  98.3 us
    ppermute x4, waiting for transfers between devices, close_floor(): m_next = lax.ppermute(m_next, peer_axis, heap)  52.6 us
    psum x1, blocking collectives, per_device(): lax.psum(jnp.concatenate([grad_gain_one, grad_gain_two, router_local]), (...  39.7 us
    all_gather x1, blocking collectives, per_device(): lax.all_gather(norm_attn, 'fsdp', axis=0, tiled=True)  36.3 us
    ppermute x4, waiting for transfers between devices, plane_reduce(): lax.ppermute(jnp.stack([to_y[half:], to_d[half:]]).astype(jnp.bfloat16),...  29.8 us
    ppermute x4, waiting for transfers between devices, plane_reduce(): lax.ppermute(pass_a.astype(jnp.bfloat16), 'fsdp', swap_pairs(4, 8))  27.9 us
    unnamed x115, local copies, waits for them, and re-layouts  21.8 us
    add x4, other arithmetic, plane_reduce(): chip = keep + got.astype(jnp.float32)  18 us
  transfers between devices with their start and end apart: 31, of which 14 were waited for; matrix products, arithmetic and copies ran while one was open for 42% of the time, Pallas kernels for 0%

profile of v1, /device:TPU:0, one launch (start us, length us, event | category | flops | bytes accessed | tf_op | source)
XLA Modules:
  0.0 653.8 jit_solution(10631853594913414510)
XLA Ops:
  20.3 9.5 %fusion.12 = f32[512,1024]{1,0:T(8,128)} fusion(bf16[4096,1024]{1,0:T(8,128)(2,1)} %param.12, s32[512]{0:T(512)S(1)} %copy-done.24), kind=kOutput, calls=%fused_computation.28 | convolution fusion | flops 4297064448 | bytes 10487808 | tf_op jit(solution)/shard_map/dot_general | solution.py:204
  29.9 12.1 %collective-permute-done = bf16[128,4096]{1,0:T(8,128)(2,1)} collective-permute-done((bf16[128,4096]{1,0:T(8,128)(2,1)}, bf16[128,4096]{1,0:T(8,128)(2,1)}, u32[]{:S(2)}, u32[]{:S(2)}) %collective-permute-start) | collective-permute-done | bytes 1048608 | tf_op jit(solution)/shard_map/ppermute | solution.py:25
  52.1 36.3 %all-gather = bf16[8,1,128]{2,1,0:T(2,128)(2,1)S(1)} all-gather(bf16[1,1,128]{2,1,0:T(2,128)(2,1)S(1)} %bitcast.194), channel_id=1, replica_groups=mesh['fsdp'=8,'dp'=4] {'fsdp'}, dimensions={0}, use_global_device_ids=true | all-gather | bytes 2304 | tf_op jit(solution)/shard_map/all_gather | solution.py:158
  88.4 9.0 %all-gather.1 = bf16[8,1,128]{2,1,0:T(2,128)(2,1)S(1)} all-gather(bf16[1,1,128]{2,1,0:T(2,128)(2,1)S(1)} %bitcast.195), channel_id=1, replica_groups=mesh['fsdp'=8,'dp'=4] {'fsdp'}, dimensions={0}, use_global_device_ids=true | all-gather | bytes 2304 | tf_op jit(solution)/shard_map/all_gather | solution.py:163
  106.9 19.1 %collective-permute-done.4 = bf16[128,4096]{1,0:T(8,128)(2,1)S(1)} collective-permute-done((bf16[128,4096]{1,0:T(8,128)(2,1)}, bf16[128,4096]{1,0:T(8,128)(2,1)S(1)}, u32[]{:S(2)}, u32[]{:S(2)}) %collective-permute-start.4) | collective-permute-done | bytes 1048608 | tf_op jit(solution)/shard_map/ppermute | solution.py:25
  130.7 21.4 %collective-permute-done.6 = bf16[128,4096]{1,0:T(8,128)(2,1)S(1)} collective-permute-done((bf16[128,4096]{1,0:T(8,128)(2,1)S(1)}, bf16[128,4096]{1,0:T(8,128)(2,1)S(1)}, u32[]{:S(2)}, u32[]{:S(2)}) %collective-permute-start.6) | collective-permute-done | bytes 1048608 | tf_op jit(solution)/shard_map/ppermute | solution.py:25
  166.5 8.6 %fusion.1 = (f32[16,512]{1,0:T(8,128)S(1)}, f32[16,512,512]{1,2,0:T(8,128)}) fusion(pred[512,512]{0,1:T(8,128)(4,1)S(1)} %compare_and_fusion, bf16[512,16,64]{0,2,1:T(8,128)(2,1)} %bitcast.161, bf16[512,16,64]{0,2,1:T(8,128)(2,1)S(1)} %bitcast.159), kind=kOutput, calls=%fused_computation.11 | convolution fusion | flops 549445632 | bytes 19169280 | tf_op jit(solution)/shard_map/qhd,khd->hqk/dot_general | solution.py:52
  175.1 9.3 %fusion = f32[16,512]{1,0:T(8,128)S(1)} fusion(f32[16,512,512]{1,2,0:T(8,128)} %get-tuple-element.61, f32[16,512]{1,0:T(8,128)S(1)} %get-tuple-element.60, pred[512,512]{0,1:T(8,128)(4,1)S(1)} %compare_and_fusion), kind=kLoop, calls=%fused_computation.8 | loop fusion | flops 16769024 | bytes 17104896 | tf_op jit(solution)/shard_map/reduce_sum | solution.py:183
  184.4 9.2 %fusion.26 = bf16[16,64,512]{2,1,0:T(8,128)(2,1)} fusion(bf16[512,16,64]{0,2,1:T(8,128)(2,1)} %bitcast.175, f32[16,512,512]{1,2,0:T(8,128)} %get-tuple-element.61, f32[16,512]{1,0:T(8,128)S(1)} %fusion, f32[16,512]{1,0:T(8,128)S(1)} %get-tuple-element.60, pred[512,512]{0,1:T(8,128)(4,1)S(1)} %compare_and_fusion), kind=kOutput, calls=%fused_computation.68 | convolution fusion | flops 558366720 | bytes 19202048 | tf_op jit(solution)/shard_map/hqk,khd->qhd/dot_general | solution.py:186
  198.2 11.7 %fusion.96 = f32[512,4096]{1,0:T(8,128)} fusion(bf16[1024,4096]{1,0:T(8,128)(2,1)} %constant_dynamic-update-slice_fusion, f32[512,1024]{1,0:T(8,128)S(1)} %get-tuple-element.18, f32[1024]{0:T(1024)S(1)} %bitcast.184, f32[512]{0:T(512)S(1)} %fusion.85), kind=kOutput, calls=%fused_computation.189 | convolution fusion | flops 4296540160 | bytes 18880512 | tf_op jit(solution)/shard_map/dot_general | solution.py:194
  209.8 8.2 %fusion.93 = f32[4096,1024]{1,0:T(8,128)S(1)} fusion(f32[512,1024]{1,0:T(8,128)S(1)} %copy-done.51, f32[512]{0:T(512)S(1)} %bitcast.189, f32[512,4096]{1,0:T(8,128)} %fusion.96), kind=kOutput, calls=%fused_computation.186 | convolution fusion | flops 4314890240 | bytes 27265024 | tf_op jit(solution)/shard_map/kf,kd->fd/dot_general | solution.py:208
  226.6 14.7 %fusion.8 = bf16[512,4096]{1,0:T(8,128)(2,1)} fusion(f32[512,4096]{1,0:T(8,128)} %fusion.96, bf16[4096,1024]{1,0:T(8,128)(2,1)} %all-gather.10.cloned.1.call-done, f32[512,1024]{1,0:T(8,128)} %fusion.12, f32[512]{0:T(512)S(1)} %bitcast.190), kind=kOutput, calls=%fused_computation.18 | convolution fusion | flops 4337958912 | bytes 23070720 | tf_op jit(solution)/shard_map/kd,fd->kf/dot_general | solution.py:212
  241.3 11.5 %multiply_reduce_fusion.1 = (f32[1024]{0:T(1024)}, f32[512]{0:T(512)S(1)}, f32[512,1024]{1,0:T(8,128)}) fusion(f32[512,1024]{1,0:T(8,128)S(1)} %copy-done.13, f32[512]{0:T(512)S(1)} %fusion.85, f32[1024]{0:T(1024)S(1)} %bitcast.185, bf16[512,4096]{1,0:T(8,128)(2,1)} %fusion.8, bf16[1024,4096]{1,0:T(8,128)(2,1)} %constant_dynamic-update-slice_fusion), kind=kOutput, calls=%fused_computation.49 | convolution fusion | flops 4298111488 | bytes 16789504 | tf_op jit(solution)/shard_map/kf,df->kd/dot_general | solution.py:221
  252.9 9.9 %multiply_reduce_fusion.3 = (f32[512]{0:T(512)S(1)}, bf16[512,1024]{1,0:T(8,128)(2,1)S(1)}, f32[512,1024]{1,0:T(8,128)}) fusion(f32[512,1024]{1,0:T(8,128)S(1)} %copy-done.52, f32[512,1024]{1,0:T(8,128)S(1)} %copy-done.13, f32[512]{0:T(512)S(1)} %multiply_multiply_fusion.3, f32[512]{0:T(512)S(1)} %fusion.85, f32[512,1024]{1,0:T(8,128)} %get-tuple-element.63, ...), kind=kOutput, calls=%fused_computation.54 | convolution fusion | flops 4319608320 | bytes 28323840 | tf_op jit(solution)/shard_map/dot_general | solution.py:197
  268.3 12.8 %multiply_reduce_fusion = (f32[16,512]{1,0:T(8,128)S(1)}, f32[16,512,512]{1,2,0:T(8,128)}) fusion(f32[16,512]{1,0:T(8,128)S(1)} %log_add_fusion, f32[16,512,512]{1,2,0:T(8,128)} %get-tuple-element.61, pred[512,512]{0,1:T(8,128)(4,1)S(1)} %compare_and_fusion, bf16[512,16,64]{0,2,1:T(8,128)(2,1)} %bitcast.177, bf16[512,16,64]{0,2,1:T(8,128)(2,1)} %bitcast.176), kind=kOutput, calls=%fused_computation.2 | convolution fusion | flops 562028544 | bytes 35979264 | tf_op jit(solution)/shard_map/qhd,khd->hqk/dot_general | solution.py:236
  281.1 12.3 %multiply_convert_fusion = bf16[16,512,512]{1,2,0:T(8,128)(2,1)S(1)} fusion(f32[16,512,512]{1,2,0:T(8,128)} %get-tuple-element.66, f32[16,512]{1,0:T(8,128)S(1)} %get-tuple-element.65, f32[16,512]{1,0:T(8,128)S(1)} %log_add_fusion, f32[16,512,512]{1,2,0:T(8,128)} %get-tuple-element.61, pred[512,512]{0,1:T(8,128)(4,1)S(1)} %compare_and_fusion), kind=kLoop, calls=%fused_computation.1 | loop fusion | flops 29360128 | bytes 42270720 | tf_op jit(solution)/shard_map/convert_element_type | solution.py:240
  314.9 10.4 %fusion.27 = bf16[16,64,512]{2,1,0:T(8,128)(2,1)S(1)} fusion(bf16[512,16,64]{0,2,1:T(8,128)(2,1)} %bitcast.178, f32[16,512]{1,0:T(8,128)S(1)} %log_add_fusion, f32[16,512,512]{1,2,0:T(8,128)} %get-tuple-element.61, pred[512,512]{0,1:T(8,128)(4,1)S(1)} %compare_and_fusion), kind=kOutput, calls=%fused_computation.70 | convolution fusion | flops 558366720 | bytes 19169280 | tf_op jit(solution)/shard_map/hqk,qhd->khd/dot_general | solution.py:250
  370.3 21.8 %collective-permute-done.14 = bf16[64,1024]{1,0:T(8,128)(2,1)S(1)} collective-permute-done((bf16[64,1024]{1,0:T(8,128)(2,1)S(1)}, bf16[64,1024]{1,0:T(8,128)(2,1)S(1)}, u32[]{:S(2)}, u32[]{:S(2)}) %collective-permute-start.14) | collective-permute-done | bytes 131104 | tf_op jit(solution)/shard_map/ppermute | solution.py:123
  392.6 39.7 %psum.39 = f32[3072]{0:T(1024)} all-reduce(f32[3072]{0:T(1024)S(1)} %pad_maximum_fusion.15), channel_id=1, replica_groups=mesh['fsdp'=8,'dp'=4] {'fsdp','dp'}, use_global_device_ids=true, to_apply=%region_16.17 | all-reduce | flops 3072 | bytes 24576 | tf_op jit(solution)/shard_map/psum | solution.py:273
  466.9 9.1 %collective-permute-done.10 = bf16[2,64,3072]{2,1,0:T(8,128)(2,1)} collective-permute-done((bf16[2,64,3072]{2,1,0:T(8,128)(2,1)S(1)}, bf16[2,64,3072]{2,1,0:T(8,128)(2,1)}, u32[]{:S(2)}, u32[]{:S(2)}) %collective-permute-start.10) | collective-permute-done | bytes 786464 | tf_op jit(solution)/shard_map/ppermute | solution.py:116
  482.1 16.2 %collective-permute-done.20 = bf16[2,64,4096]{2,1,0:T(8,128)(2,1)S(1)} collective-permute-done((bf16[2,64,4096]{2,1,0:T(8,128)(2,1)S(1)}, bf16[2,64,4096]{2,1,0:T(8,128)(2,1)S(1)}, u32[]{:S(2)}, u32[]{:S(2)}) %collective-permute-start.20) | collective-permute-done | bytes 1048608 | tf_op jit(solution)/shard_map/ppermute | solution.py:116
  519.2 10.0 %add_convert_fusion.1 = bf16[4096,1024]{1,0:T(8,128)(2,1)} fusion(bf16[4096,1024]{1,0:T(8,128)(2,1)} %param.11, s32[512]{0:T(512)S(1)} %copy-done.25, f32[512,1024]{1,0:T(8,128)} %get-tuple-element.64, f32[512]{0:T(512)S(1)} %bitcast.192), kind=kOutput, calls=%fused_computation.4 | convolution fusion | flops 4310695936 | bytes 18878464 | tf_op jit(solution)/shard_map/kt,kd->td/dot_general | solution.py:202
  529.3 11.6 %add_convert_fusion = bf16[4096,1024]{1,0:T(8,128)(2,1)} fusion(bf16[4096,1024]{1,0:T(8,128)(2,1)} %param.12, s32[512]{0:T(512)S(1)} %copy-done.25, f32[512,1024]{1,0:T(8,128)S(1)} %get-tuple-element.59, f32[512,1024]{1,0:T(8,128)S(1)} %copy-done.53, f32[1024]{0:T(1024)S(1)} %copy-done.29, f32[512]{0:T(512)S(1)} %copy-done.38, f32[512]{0:T(512)S(1)} %copy-done.41, ...), kind=kOutput, calls=%fused_computation | convolution fusion | flops 4316987392 | bytes 25190400 | tf_op jit(solution)/shard_map/kt,kd->td/dot_general | solution.py:270
  540.9 98.3 %all-reduce.3.cloned.1.call-done = (bf16[128,3072]{1,0:T(8,128)(2,1)}, bf16[128,1024]{1,0:T(8,128)(2,1)}, bf16[128,4096]{1,0:T(8,128)(2,1)}, bf16[512,1024]{1,0:T(8,128)(2,1)}) async-done(((bf16[128,3072]{1,0:T(8,128)(2,1)}, bf16[128,1024]{1,0:T(8,128)(2,1)}, bf16[128,4096]{1,0:T(8,128)(2,1)}, bf16[512,1024]{1,0:T(8,128)(2,1)}), (bf16[128,3072]{1,0:T(8,128)(2,1)}, bf16[128,1024]{1,0:T(8,128)(2,1)}, ...) | async-done | bytes 3145744 | tf_op jit(solution)/shard_map/psum | solution.py:130
  (267 shorter events, 205.7 us)
Async XLA Ops:
  7.2 145.9 %all-gather.6.cloned.1.call-start = ((), (), s32[]{:S(2)}) async-start(), calls=%async_computation | async-start | bytes 7077888 | tf_op jit(solution)/shard_map/all_gather | solution.py:157
  7.9 185.7 %all-gather.8.cloned.1.call-start = ((), (), s32[]{:S(2)}) async-start(), calls=%async_computation.1 | async-start | bytes 2359296 | tf_op jit(solution)/shard_map/all_gather | solution.py:160
  8.7 217.9 %all-gather.10.cloned.1.call-start = ((), (), s32[]{:S(2)}) async-start(), calls=%async_computation.2 | async-start | bytes 9437184 | tf_op jit(solution)/shard_map/all_gather | solution.py:165
  8.7 33.3 %collective-permute-start = (bf16[128,4096]{1,0:T(8,128)(2,1)}, bf16[128,4096]{1,0:T(8,128)(2,1)}, u32[]{:S(2)}, u32[]{:S(2)}) collective-permute-start(bf16[128,4096]{1,0:T(8,128)(2,1)} %param.17), channel_id=1, source_target_pairs={{0,4},{4,8},{8,12},{12,16},{16,20},{20,24},{24,28},{28,0},{1,5},{5... | collective-permute-start | bytes 3145736 | tf_op jit(solution)/shard_map/ppermute | solution.py:25
  9.3 39.9 %collective-permute-start.1 = (bf16[128,4096]{1,0:T(8,128)(2,1)}, bf16[128,4096]{1,0:T(8,128)(2,1)}, u32[]{:S(2)}, u32[]{:S(2)}) collective-permute-start(bf16[128,4096]{1,0:T(8,128)(2,1)} %param.17), channel_id=1, source_target_pairs={{0,28},{4,0},{8,4},{12,8},{16,12},{20,16},{24,20},{28,24},{1,29},{... | collective-permute-start | bytes 3145736 | tf_op jit(solution)/shard_map/ppermute | solution.py:28
  12.2 627.0 %all-reduce.3.cloned.1.call-start = ((), (), s32[]{:S(2)}) async-start(), calls=%async_computation.3 | async-start | bytes 6291456 | tf_op jit(solution)/shard_map/psum | solution.py:130
  42.0 55.4 %collective-permute-start.2 = (bf16[128,4096]{1,0:T(8,128)(2,1)}, bf16[128,4096]{1,0:T(8,128)(2,1)}, u32[]{:S(2)}, u32[]{:S(2)}) collective-permute-start(bf16[128,4096]{1,0:T(8,128)(2,1)} %collective-permute-done), channel_id=1, source_target_pairs={{0,4},{4,8},{8,12},{12,16},{16,20},{20,24},{24,28},{28,0},{1,5},{5... | collective-permute-start | bytes 3145736 | tf_op jit(solution)/shard_map/ppermute | solution.py:25
  49.2 53.3 %collective-permute-start.3 = (bf16[128,4096]{1,0:T(8,128)(2,1)}, bf16[128,4096]{1,0:T(8,128)(2,1)S(1)}, u32[]{:S(2)}, u32[]{:S(2)}) collective-permute-start(bf16[128,4096]{1,0:T(8,128)(2,1)} %collective-permute-done.1), channel_id=1, source_target_pairs={{0,28},{4,0},{8,4},{12,8},{16,12},{20,16},{24,20},{28,24},{1,29},{... | collective-permute-start | bytes 3145736 | tf_op jit(solution)/shard_map/ppermute | solution.py:28
  97.4 28.6 %collective-permute-start.4 = (bf16[128,4096]{1,0:T(8,128)(2,1)}, bf16[128,4096]{1,0:T(8,128)(2,1)S(1)}, u32[]{:S(2)}, u32[]{:S(2)}) collective-permute-start(bf16[128,4096]{1,0:T(8,128)(2,1)} %collective-permute-done.2), channel_id=1, source_target_pairs={{0,4},{4,8},{8,12},{12,16},{16,20},{20,24},{24,28},{28,0},{1,5},{5... | collective-permute-start | bytes 3145736 | tf_op jit(solution)/shard_map/ppermute | solution.py:25
  102.5 27.2 %collective-permute-start.5 = (bf16[128,4096]{1,0:T(8,128)(2,1)S(1)}, bf16[128,4096]{1,0:T(8,128)(2,1)S(1)}, u32[]{:S(2)}, u32[]{:S(2)}) collective-permute-start(bf16[128,4096]{1,0:T(8,128)(2,1)S(1)} %collective-permute-done.3), channel_id=1, source_target_pairs={{0,28},{4,0},{8,4},{12,8},{16,12},{20,16},{24,20},{28,24},{1,29},{... | collective-permute-start | bytes 3145736 | tf_op jit(solution)/shard_map/ppermute | solution.py:28
  126.0 26.1 %collective-permute-start.6 = (bf16[128,4096]{1,0:T(8,128)(2,1)S(1)}, bf16[128,4096]{1,0:T(8,128)(2,1)S(1)}, u32[]{:S(2)}, u32[]{:S(2)}) collective-permute-start(bf16[128,4096]{1,0:T(8,128)(2,1)S(1)} %collective-permute-done.4), channel_id=1, source_target_pairs={{0,4},{4,8},{8,12},{12,16},{16,20},{20,24},{24,28},{28,0},{1,5},{5... | collective-permute-start | bytes 3145736 | tf_op jit(solution)/shard_map/ppermute | solution.py:25
  226.5 118.6 %collective-permute-start.22 = (bf16[4,512,1024]{2,1,0:T(8,128)(2,1)}, bf16[4,512,1024]{2,1,0:T(8,128)(2,1)}, u32[]{:S(2)}, u32[]{:S(2)}) collective-permute-start(bf16[4,512,1024]{2,1,0:T(8,128)(2,1)} %fusion.17), channel_id=1, source_target_pairs={{0,4},{4,0},{8,12},{12,8},{16,20},{20,16},{24,28},{28,24},{1,5},{5... | collective-permute-start | bytes 12582920 | tf_op jit(solution)/shard_map/ppermute | solution.py:103
  308.2 146.3 %collective-permute-start.17 = (bf16[4,128,4096]{2,1,0:T(8,128)(2,1)}, bf16[4,128,4096]{2,1,0:T(8,128)(2,1)}, u32[]{:S(2)}, u32[]{:S(2)}) collective-permute-start(bf16[4,128,4096]{2,1,0:T(8,128)(2,1)} %fusion.16), channel_id=1, source_target_pairs={{0,4},{4,0},{8,12},{12,8},{16,20},{20,16},{24,28},{28,24},{1,5},{5... | collective-permute-start | bytes 12582920 | tf_op jit(solution)/shard_map/ppermute | solution.py:103
  314.4 37.2 %collective-permute-start.12 = (bf16[4,128,1024]{2,1,0:T(8,128)(2,1)S(1)}, bf16[4,128,1024]{2,1,0:T(8,128)(2,1)}, u32[]{:S(2)}, u32[]{:S(2)}) collective-permute-start(bf16[4,128,1024]{2,1,0:T(8,128)(2,1)S(1)} %fusion.32), channel_id=1, source_target_pairs={{0,4},{4,0},{8,12},{12,8},{16,20},{20,16},{24,28},{28,24},{1,5},{5... | collective-permute-start | bytes 3145736 | tf_op jit(solution)/shard_map/ppermute | solution.py:103
  335.9 111.4 %collective-permute-start.7 = (bf16[4,128,3072]{2,1,0:T(8,128)(2,1)}, bf16[4,128,3072]{2,1,0:T(8,128)(2,1)}, u32[]{:S(2)}, u32[]{:S(2)}) collective-permute-start(bf16[4,128,3072]{2,1,0:T(8,128)(2,1)} %fusion.22), channel_id=1, source_target_pairs={{0,4},{4,0},{8,12},{12,8},{16,20},{20,16},{24,28},{28,24},{1,5},{5... | collective-permute-start | bytes 9437192 | tf_op jit(solution)/shard_map/ppermute | solution.py:103
  361.5 75.4 %collective-permute-start.25 = (bf16[2,256,1024]{2,1,0:T(8,128)(2,1)}, bf16[2,256,1024]{2,1,0:T(8,128)(2,1)}, u32[]{:S(2)}, u32[]{:S(2)}) collective-permute-start(bf16[2,256,1024]{2,1,0:T(8,128)(2,1)} %pad_maximum_fusion.7), channel_id=1, source_target_pairs={{0,16},{4,20},{8,24},{12,28},{16,0},{20,4},{24,8},{28,12},{1,17},{... | collective-permute-start | bytes 3145736 | tf_op jit(solution)/shard_map/ppermute | solution.py:116
  367.4 70.8 %collective-permute-start.23 = (bf16[2,256,1024]{2,1,0:T(8,128)(2,1)}, bf16[2,256,1024]{2,1,0:T(8,128)(2,1)}, u32[]{:S(2)}, u32[]{:S(2)}) collective-permute-start(bf16[2,256,1024]{2,1,0:T(8,128)(2,1)} %pad_maximum_fusion.6), channel_id=1, source_target_pairs={{0,8},{4,12},{8,0},{12,4},{16,24},{20,28},{24,16},{28,20},{1,9},{5... | collective-permute-start | bytes 3145736 | tf_op jit(solution)/shard_map/ppermute | solution.py:113
  368.1 24.1 %collective-permute-start.14 = (bf16[64,1024]{1,0:T(8,128)(2,1)S(1)}, bf16[64,1024]{1,0:T(8,128)(2,1)S(1)}, u32[]{:S(2)}, u32[]{:S(2)}) collective-permute-start(bf16[64,1024]{1,0:T(8,128)(2,1)S(1)} %get-tuple-element.42), channel_id=1, source_target_pairs={{0,16},{4,20},{8,24},{12,28},{16,0},{20,4},{24,8},{28,12},{1,17},{... | collective-permute-start | bytes 393224 | tf_op jit(solution)/shard_map/ppermute | solution.py:123
  392.2 42.8 %collective-permute-start.16 = (bf16[64,1024]{1,0:T(8,128)(2,1)S(1)}, bf16[64,1024]{1,0:T(8,128)(2,1)S(1)}, u32[]{:S(2)}, u32[]{:S(2)}) collective-permute-start(bf16[64,1024]{1,0:T(8,128)(2,1)S(1)} %get-tuple-element.43), channel_id=1, source_target_pairs={{0,8},{4,12},{8,0},{12,4},{16,24},{20,28},{24,16},{28,20},{1,9},{5... | collective-permute-start | bytes 393224 | tf_op jit(solution)/shard_map/ppermute | solution.py:126
  452.7 25.3 %collective-permute-start.8 = (bf16[2,64,3072]{2,1,0:T(8,128)(2,1)S(1)}, bf16[2,64,3072]{2,1,0:T(8,128)(2,1)}, u32[]{:S(2)}, u32[]{:S(2)}) collective-permute-start(bf16[2,64,3072]{2,1,0:T(8,128)(2,1)S(1)} %pad_maximum_fusion.9), channel_id=1, source_target_pairs={{0,8},{4,12},{8,0},{12,4},{16,24},{20,28},{24,16},{28,20},{1,9},{5... | collective-permute-start | bytes 2359304 | tf_op jit(solution)/shard_map/ppermute | solution.py:113
  460.8 37.5 %collective-permute-start.20 = (bf16[2,64,4096]{2,1,0:T(8,128)(2,1)S(1)}, bf16[2,64,4096]{2,1,0:T(8,128)(2,1)S(1)}, u32[]{:S(2)}, u32[]{:S(2)}) collective-permute-start(bf16[2,64,4096]{2,1,0:T(8,128)(2,1)S(1)} %pad_maximum_fusion.4), channel_id=1, source_target_pairs={{0,16},{4,20},{8,24},{12,28},{16,0},{20,4},{24,8},{28,12},{1,17},{... | collective-permute-start | bytes 3145736 | tf_op jit(solution)/shard_map/ppermute | solution.py:116
  461.7 38.7 %collective-permute-start.18 = (bf16[2,64,4096]{2,1,0:T(8,128)(2,1)S(1)}, bf16[2,64,4096]{2,1,0:T(8,128)(2,1)S(1)}, u32[]{:S(2)}, u32[]{:S(2)}) collective-permute-start(bf16[2,64,4096]{2,1,0:T(8,128)(2,1)S(1)} %pad_maximum_fusion.3), channel_id=1, source_target_pairs={{0,8},{4,12},{8,0},{12,4},{16,24},{20,28},{24,16},{28,20},{1,9},{5... | collective-permute-start | bytes 3145736 | tf_op jit(solution)/shard_map/ppermute | solution.py:113
  479.5 29.3 %collective-permute-start.11 = (bf16[64,3072]{1,0:T(8,128)(2,1)S(1)}, bf16[64,3072]{1,0:T(8,128)(2,1)S(1)}, u32[]{:S(2)}, u32[]{:S(2)}) collective-permute-start(bf16[64,3072]{1,0:T(8,128)(2,1)S(1)} %get-tuple-element.34), channel_id=1, source_target_pairs={{0,8},{4,12},{8,0},{12,4},{16,24},{20,28},{24,16},{28,20},{1,9},{5... | collective-permute-start | bytes 1179656 | tf_op jit(solution)/shard_map/ppermute | solution.py:126
  480.8 28.0 %collective-permute-start.9 = (bf16[64,3072]{1,0:T(8,128)(2,1)S(1)}, bf16[64,3072]{1,0:T(8,128)(2,1)S(1)}, u32[]{:S(2)}, u32[]{:S(2)}) collective-permute-start(bf16[64,3072]{1,0:T(8,128)(2,1)S(1)} %get-tuple-element.33), channel_id=1, source_target_pairs={{0,16},{4,20},{8,24},{12,28},{16,0},{20,4},{24,8},{28,12},{1,17},{... | collective-permute-start | bytes 1179656 | tf_op jit(solution)/shard_map/ppermute | solution.py:123
  (64 other events, 1426.1 us)
Sparse Core Ops, SparseCore 0:
  9.9 70.1 all-gather.5
  81.9 33.4 all-gather.7
  117.3 60.3 all-gather.9
  519.2 120.0 all-reduce.2
